TPU v7x, 256 devices: a whole 4x4x8 slice. The times are simulated.
256 devices in a mesh: dp: 32 (over x, z_hi, core), tensor: 8 (over y, z_lo).
Axes of the slice: x: 4, y: 4, z: 8 (z_hi: 4, z_lo: 2; z = z_hi * 2 + z_lo), core: 2. Of those that a mesh axis runs over, the one named last changes fastest.
Arguments:
- stream: bfloat16 [64, 430, 2048], P('dp', None, 'tensor'), may hold values from -3 to 3
- normed: bfloat16 [64, 430, 2048], P('dp'), may hold values from -6 to 6
- query_weight: bfloat16 [2048, 2048], P(None, 'tensor'), as said below
- key_weight: bfloat16 [2048, 2048], P(None, 'tensor'), as said below
- value_weight: bfloat16 [2048, 2048], P(None, 'tensor'), may hold values from -0.125 to 0.125
- out_weight: bfloat16 [2048, 2048], P('tensor'), may hold values from -0.125 to 0.125
- norm_gain: bfloat16 [2048], P('tensor'), may hold values from 0.099609375 to 1.8984375
- proj_weight: bfloat16 [2048, 1024], P('tensor'), may hold values from -0.125 to 0.125
- images: bfloat16 [64, 1024], P('dp'), may hold values from -6 to 6
Outputs:
- mean_loss: float32 [], replicated
- grad_normed: bfloat16 [64, 430, 2048], P('dp', None, 'tensor')
- grad_query: float32 [2048, 2048], P('dp', 'tensor')
- grad_key: float32 [2048, 2048], P('dp', 'tensor')
- grad_value: float32 [2048, 2048], P('dp', 'tensor')
- grad_out: float32 [2048, 2048], P('tensor', 'dp')
- grad_proj: float32 [2048, 1024], P('tensor', 'dp')
Inputs may be any that keep to these rules, and one draw needn't show every extreme that they name: `query_weight`: query projection entries, independent draws of order 2048^-0.5. `key_weight`: key projection entries, of order 2048^-0.5, in some heads up to about sixteen times that, possibly aligned with the query projection.
All inputs are finite; a program needn't handle non-finite values.
Results may differ from a plain program's by a relative error of at most 0.02.
Values may be sent and summed in bfloat16 or wider, within the bound.
No kernel may reach another device: no remote copies, remote signals or barrier semaphores. Data moves between devices by JAX's collectives and lax.ppermute only.
A program may use at most 128 MiB of HBM per device.

v0:
```python
import jax
import jax.numpy as jnp
from jax import lax
from jax.sharding import PartitionSpec as P

D = 2048
H = 16
SCALE_LOGIT = 14.0
GRAD_SCALE = 256.0
EPSILON = 1e-05
HIGH = lax.Precision.HIGHEST


def project(inputs, weight):
    return jnp.einsum("bld,dc->blc", inputs, weight, preferred_element_type=jnp.float32).astype(
        jnp.bfloat16
    )


def split_heads(values, head_size):
    return values.reshape(values.shape[0], values.shape[1], values.shape[2] // head_size, head_size)


def local(
    stream,
    normed,
    query_weight,
    key_weight,
    value_weight,
    out_weight,
    norm_gain,
    proj_weight,
    images,
):
    seq_count = normed.shape[0]
    length = normed.shape[1]
    col_count = query_weight.shape[1]
    feat_share = stream.shape[2]
    head_size = D // H
    scale_head = head_size ** (-0.5)
    queries = split_heads(project(normed, query_weight), head_size)
    keys_all = split_heads(project(normed, key_weight), head_size)
    values_all = split_heads(project(normed, value_weight), head_size)
    scores = (
        jnp.einsum("bqhd,bkhd->bhqk", queries, keys_all, preferred_element_type=jnp.float32)
        * scale_head
    )
    row_max = jnp.max(scores, axis=-1, keepdims=True)
    exp_scores = jnp.exp(scores - row_max)
    attn_prob = exp_scores / jnp.sum(exp_scores, axis=-1, keepdims=True)
    attn_half = attn_prob.astype(jnp.bfloat16)
    heads_out = jnp.einsum(
        "bhqk,bkhd->bqhd", attn_half, values_all, preferred_element_type=jnp.float32
    )
    head_concat = heads_out.astype(jnp.bfloat16).reshape(seq_count, length, col_count)
    partial_value = jnp.einsum(
        "blc,cd->bld", head_concat, out_weight, preferred_element_type=jnp.float32
    )
    summed = lax.psum(partial_value.astype(jnp.bfloat16), "tensor").astype(jnp.float32)
    attended = lax.dynamic_slice_in_dim(
        summed, lax.axis_index("tensor") * feat_share, feat_share, 2
    )
    residual = stream.astype(jnp.float32) + attended
    center = lax.psum(jnp.sum(residual, axis=-1), "tensor") / D
    offset = residual - center[..., None]
    variance = lax.psum(jnp.sum(offset * offset, axis=-1), "tensor") / D
    inv_std = lax.rsqrt(variance + EPSILON)[..., None]
    normal_feat = (residual - center[..., None]) * inv_std
    gain_float = norm_gain.astype(jnp.float32)
    pooled = jnp.mean(normal_feat * gain_float, axis=1).astype(jnp.bfloat16)
    embedded = lax.psum(jnp.dot(pooled, proj_weight, preferred_element_type=jnp.float32), "tensor")
    embed_norm = jnp.sqrt(jnp.sum(embedded * embedded, axis=-1, keepdims=True) + EPSILON)
    spectra = embedded / embed_norm
    gathered = lax.all_gather(images, "dp", axis=0, tiled=True).astype(jnp.float32)
    image_unit = gathered / jnp.sqrt(jnp.sum(gathered * gathered, axis=-1, keepdims=True) + EPSILON)
    logits = SCALE_LOGIT * jnp.dot(spectra, image_unit.T, precision=HIGH)
    own_start = lax.axis_index("dp") * seq_count
    columns = jnp.arange(logits.shape[1], dtype=jnp.int32)
    own_rows = own_start + jnp.arange(seq_count, dtype=jnp.int32)
    matches = (columns[None, :] == own_rows[:, None]).astype(jnp.float32)
    exp_logits = jnp.exp(logits)
    row_lse = jnp.log(jnp.sum(exp_logits, axis=1))
    diagonal = jnp.sum(logits * matches, axis=1)
    local_loss = 0.5 * jnp.sum(row_lse) - jnp.sum(diagonal)
    col_total, loss_sum = lax.psum((jnp.sum(exp_logits, axis=0), local_loss), "dp")
    col_lse = jnp.log(col_total)
    mean_loss = (loss_sum + 0.5 * jnp.sum(col_lse)) / logits.shape[1]
    grad_logits = GRAD_SCALE * (
        0.5 * jnp.exp(logits - row_lse[:, None])
        + 0.5 * jnp.exp(logits - col_lse[None, :])
        - matches
    )
    grad_spec = SCALE_LOGIT * jnp.dot(grad_logits, image_unit, precision=HIGH)
    radial = jnp.sum(spectra * grad_spec, axis=-1, keepdims=True)
    grad_embed = ((grad_spec - spectra * radial) / embed_norm).astype(jnp.bfloat16)
    grad_proj = lax.dot_general(
        pooled, grad_embed, (((0,), (0,)), ((), ())), preferred_element_type=jnp.float32
    )
    grad_pooled = lax.dot_general(
        grad_embed, proj_weight, (((1,), (1,)), ((), ())), preferred_element_type=jnp.float32
    )
    grad_normal = jnp.broadcast_to(grad_pooled[:, None, :] / length, normal_feat.shape) * gain_float
    mean_one, mean_two = lax.psum(
        (jnp.sum(grad_normal, axis=-1), jnp.sum(grad_normal * normal_feat, axis=-1)), "tensor"
    )
    grad_resid = (
        inv_std * (grad_normal - mean_one[..., None] / D - normal_feat * (mean_two[..., None] / D))
    ).astype(jnp.bfloat16)
    piece_rows = lax.all_gather(grad_resid, "tensor", axis=2, tiled=True)
    grad_heads = jnp.einsum(
        "blw,cw->blc", piece_rows, out_weight, preferred_element_type=jnp.float32
    )
    update = jnp.einsum("blc,blw->cw", head_concat, piece_rows, preferred_element_type=jnp.float32)
    grad_out = update
    grad_heads, grad_out = (grad_heads, grad_out)
    grad_heads = split_heads(grad_heads.astype(jnp.bfloat16), head_size)
    grad_probs = jnp.einsum(
        "bqhd,bkhd->bhqk", grad_heads, values_all, preferred_element_type=jnp.float32
    )
    row_dot = jnp.sum(attn_prob * grad_probs, axis=-1, keepdims=True)
    grad_scores = (attn_prob * (grad_probs - row_dot) * scale_head).astype(jnp.bfloat16)
    grad_q = (
        jnp.einsum("bhqk,bkhd->bqhd", grad_scores, keys_all, preferred_element_type=jnp.float32)
        .astype(jnp.bfloat16)
        .reshape(seq_count, length, col_count)
    )
    grad_k = (
        jnp.einsum("bhqk,bqhd->bkhd", grad_scores, queries, preferred_element_type=jnp.float32)
        .astype(jnp.bfloat16)
        .reshape(seq_count, length, col_count)
    )
    grad_v = (
        jnp.einsum("bhqk,bqhd->bkhd", attn_half, grad_heads, preferred_element_type=jnp.float32)
        .astype(jnp.bfloat16)
        .reshape(seq_count, length, col_count)
    )
    back_input = jnp.einsum("blc,dc->bld", grad_q, query_weight, preferred_element_type=jnp.float32)
    back_input = back_input + jnp.einsum(
        "blc,dc->bld", grad_k, key_weight, preferred_element_type=jnp.float32
    )
    back_input = back_input + jnp.einsum(
        "blc,dc->bld", grad_v, value_weight, preferred_element_type=jnp.float32
    )
    grad_normed = lax.psum_scatter(
        back_input.astype(jnp.bfloat16), "tensor", scatter_dimension=2, tiled=True
    )
    grad_query = jnp.einsum("bld,blc->dc", normed, grad_q, preferred_element_type=jnp.float32)
    grad_key = jnp.einsum("bld,blc->dc", normed, grad_k, preferred_element_type=jnp.float32)
    grad_value = jnp.einsum("bld,blc->dc", normed, grad_v, preferred_element_type=jnp.float32)
    reduced = (
        lax.psum_scatter(
            grad_query.astype(jnp.bfloat16), "dp", scatter_dimension=0, tiled=True
        ).astype(jnp.float32),
        lax.psum_scatter(
            grad_key.astype(jnp.bfloat16), "dp", scatter_dimension=0, tiled=True
        ).astype(jnp.float32),
        lax.psum_scatter(
            grad_value.astype(jnp.bfloat16), "dp", scatter_dimension=0, tiled=True
        ).astype(jnp.float32),
        lax.psum_scatter(
            grad_out.astype(jnp.bfloat16), "dp", scatter_dimension=1, tiled=True
        ).astype(jnp.float32),
        lax.psum_scatter(
            grad_proj.astype(jnp.bfloat16), "dp", scatter_dimension=1, tiled=True
        ).astype(jnp.float32),
    )
    return (mean_loss, grad_normed, reduced[0], reduced[1], reduced[2], reduced[3], reduced[4])


def solution(mesh):
    return jax.shard_map(
        local,
        mesh=mesh,
        in_specs=(
            P("dp", None, "tensor"),
            P("dp", None, None),
            P(None, "tensor"),
            P(None, "tensor"),
            P(None, "tensor"),
            P("tensor", None),
            P("tensor"),
            P("tensor", None),
            P("dp", None),
        ),
        out_specs=(
            P(),
            P("dp", None, "tensor"),
            P("dp", "tensor"),
            P("dp", "tensor"),
            P("dp", "tensor"),
            P("tensor", "dp"),
            P("tensor", "dp"),
        ),
        check_vma=False,
    )
```

profile of v0, /device:TPU:1, one launch (start us, length us, event | category | flops | bytes accessed | tf_op | source)
XLA Modules:
  0.0 972.7 jit_solution(16875496119188521870)
XLA Ops:
  7.2 4.5 fusion.42
  11.9 4.0 fusion.45
  16.0 4.3 fusion.39
  20.5 0.6 fusion.81
  21.2 2.8 fusion.122
  24.0 4.7 fusion.48
  28.7 0.3 copy.70
  29.0 0.3 reshape.74
  29.4 3.0 convolution_convert_fusion
  32.5 50.5 %all-gather = bf16[32,2,1024]{2,1,0:T(2,128)(2,1)S(1)} all-gather(bf16[1,2,1024]{2,1,0:T(2,128)(2,1)S(1)} %bitcast.72), channel_id=1, replica_groups=mesh['dp'=32,'tensor'=8] {'dp'}, dimensions={0}, use_global_device_ids=true | all-gather | bytes 135168 | tf_op jit(solution)/shard_map/all_gather | solution.py:74
  83.2 117.2 %all-reduce.4.cloned.1.call-done = bf16[2,430,2048]{2,1,0:T(8,128)(2,1)} async-done(((bf16[2,430,2048]{2,1,0:T(8,128)(2,1)}), bf16[2,430,2048]{2,1,0:T(8,128)(2,1)}) %all-reduce.4.cloned.1.call-update) | async-done | bytes 3522576 | tf_op jit(solution)/shard_map/psum | solution.py:59
  200.4 1.2 fusion.73
  201.6 12.8 %psum.57 = f32[2,430]{1,0:T(2,128)S(1)} all-reduce(f32[2,430]{1,0:T(2,128)S(1)} %fusion.73), channel_id=1, replica_groups=mesh['dp'=32,'tensor'=8] {'tensor'}, use_global_device_ids=true, to_apply=%region_4.0 | all-reduce | flops 860 | bytes 6880 | tf_op jit(solution)/shard_map/psum | solution.py:64
  214.4 1.4 multiply_reduce_fusion.4
  215.8 13.8 %psum.58 = f32[2,430]{1,0:T(2,128)S(1)} all-reduce(f32[2,430]{1,0:T(2,128)S(1)} %multiply_reduce_fusion.4), channel_id=1, replica_groups=mesh['dp'=32,'tensor'=8] {'tensor'}, use_global_device_ids=true, to_apply=%region_6.0 | all-reduce | flops 860 | bytes 6880 | tf_op jit(solution)/shard_map/psum | solution.py:66
  229.7 1.3 multiply_reduce_fusion.3
  231.2 13.3 %psum.59 = f32[2,1024]{1,0:T(2,128)S(1)} all-reduce(f32[2,1024]{1,0:T(2,128)S(1)} %fusion.102), channel_id=1, replica_groups=mesh['dp'=32,'tensor'=8] {'tensor'}, use_global_device_ids=true, to_apply=%region_8.0 | all-reduce | flops 2048 | bytes 16384 | tf_op jit(solution)/shard_map/psum | solution.py:71
  244.6 1.0 exponential_reduce_fusion
  245.6 0.6 fusion.120
  247.5 83.0 %all-reduce = (f32[64]{0:T(128)S(1)}, f32[]{:T(128)}) all-reduce(f32[64]{0:T(128)S(1)} %get-tuple-element.30, f32[]{:T(128)S(6)} %sub.68), channel_id=1, replica_groups=mesh['dp'=32,'tensor'=8] {'dp'}, use_global_device_ids=true, to_apply=%region_16.0 | all-reduce | flops 65 | bytes 520 | tf_op jit(solution)/shard_map/psum | solution.py:85
  330.6 0.6 fusion.121
  331.2 0.4 multiply_reduce_fusion.6
  331.9 1.6 multiply_reduce_fusion.2
  333.5 13.0 %all-reduce.1 = (f32[2,430]{1,0:T(2,128)S(1)}, f32[2,430]{1,0:T(2,128)S(1)}) all-reduce(f32[2,430]{1,0:T(2,128)S(1)} %get-tuple-element.29, f32[2,430]{1,0:T(2,128)S(1)} %get-tuple-element.28), channel_id=1, replica_groups=mesh['dp'=32,'tensor'=8] {'tensor'}, use_global_device_ids=true, to_apply=%region_22.0 | all-reduce | flops 1720 | bytes 13760 | tf_op jit(solution)/shard_map/psum | solution.py:103
  346.5 2.3 fusion.68
  349.0 1.3 convolution_convert_fusion.1
  350.3 73.9 %all-gather.3.cloned.1.call-done = bf16[2,430,2048]{2,1,0:T(8,128)(2,1)} async-done(((bf16[2,430,256]{2,1,0:T(8,128)(2,1)}), bf16[2,430,2048]{2,1,0:T(8,128)(2,1)}) %all-gather.3.cloned.1.call-update) | async-done | bytes 3522576 | tf_op jit(solution)/shard_map/all_gather | solution.py:109
  424.2 3.1 convolution_convert_fusion.3
  427.5 4.5 fusion.49
  432.0 0.3 copy.79
  432.4 0.3 reshape.78
  432.6 4.4 fusion.12
  437.1 1.3 copy.93
  438.6 3.6 fusion.76
  442.2 6.6 fusion.50
  448.9 0.3 copy.77
  449.2 0.3 reshape.77
  449.5 4.4 fusion.13
  453.9 1.3 copy.91
  455.3 7.0 fusion.53
  462.3 0.3 copy.75
  462.7 0.3 reshape.76
  462.9 4.4 fusion.14
  467.4 1.3 copy.89
  468.8 4.9 fusion.11
  473.7 0.3 reduce-scatter.13.cloned.1.call-start
  474.0 1.1 fusion.61
  475.2 1.1 fusion.58
  476.4 2.9 add_convert_fusion
  480.7 35.0 %reduce-scatter.17.cloned.1.call-done = bf16[256,32]{0,1:T(8,128)(2,1)} async-done(((bf16[256,1024]{0,1:T(8,128)(2,1)}), bf16[256,32]{0,1:T(8,128)(2,1)}) %reduce-scatter.17.cloned.1.call-update) | async-done | bytes 16400 | tf_op jit(solution)/shard_map/reduce_scatter | solution.py:163
  515.7 1.3 convert_element_type.147
  517.1 89.3 %reduce-scatter.23.cloned.1.call-done = bf16[64,256]{1,0:T(8,128)(2,1)} async-done(((bf16[2048,256]{1,0:T(8,128)(2,1)}), bf16[64,256]{1,0:T(8,128)(2,1)}) %reduce-scatter.23.cloned.1.call-update) | async-done | bytes 32784
  606.4 0.9 copy.94
  607.3 0.7 copy.86
  608.0 89.1 %reduce-scatter.21.cloned.1.call-done = bf16[64,256]{1,0:T(8,128)(2,1)} async-done(((bf16[2048,256]{1,0:T(8,128)(2,1)}), bf16[64,256]{1,0:T(8,128)(2,1)}) %reduce-scatter.21.cloned.1.call-update) | async-done | bytes 32784
  697.1 0.9 copy.92
  698.0 0.7 copy.85
  698.7 89.1 %reduce-scatter.19.cloned.1.call-done = bf16[64,256]{1,0:T(8,128)(2,1)} async-done(((bf16[2048,256]{1,0:T(8,128)(2,1)}), bf16[64,256]{1,0:T(8,128)(2,1)}) %reduce-scatter.19.cloned.1.call-update) | async-done | bytes 32784
  787.8 0.9 copy.90
  788.7 0.7 copy.84
  789.4 89.2 %reduce-scatter.15.cloned.1.call-done = bf16[256,64]{0,1:T(8,128)(2,1)} async-done(((bf16[256,2048]{0,1:T(8,128)(2,1)}), bf16[256,64]{0,1:T(8,128)(2,1)}) %reduce-scatter.15.cloned.1.call-update) | async-done | bytes 32784 | tf_op jit(solution)/shard_map/reduce_scatter | solution.py:160
  878.6 1.4 convert_element_type.145
  880.0 82.3 %reduce-scatter.13.cloned.1.call-done = bf16[2,430,256]{2,1,0:T(8,128)(2,1)} async-done(((bf16[2,430,2048]{2,1,0:T(8,128)(2,1)}), bf16[2,430,256]{2,1,0:T(8,128)(2,1)}) %reduce-scatter.13.cloned.1.call-update) | async-done | bytes 440336 | tf_op jit(solution)/shard_map/reduce_scatter | solution.py:144
  962.4 2.1 copy.83
  (57 shorter events, 2.1 us)
Async XLA Ops:
  7.2 22.2 %copy-start = (bf16[256,2048]{1,0:T(8,128)(2,1)S(1)}, bf16[256,2048]{1,0:T(8,128)(2,1)}, u32[]{:S(2)}) copy-start(bf16[256,2048]{1,0:T(8,128)(2,1)} %param.14) | copy-start | bytes 3145732
  7.2 4.7 copy-start.7
  7.2 193.2 %all-reduce.4.cloned.1.call-start = ((), (), s32[]{:S(2)}) async-start(), calls=%async_computation.6 | async-start | bytes 7077888 | tf_op jit(solution)/shard_map/psum | solution.py:59
  20.5 3.5 copy-start.3
  21.2 2.8 copy-start.1
  29.3 3.0 copy-start.5
  29.4 3.1 copy-start.12
  29.4 3.1 copy-start.11
  29.4 171.0 %copy-start.2 = (bf16[2,430,256]{2,0,1:T(2,128)(2,1)S(1)}, bf16[2,430,256]{2,0,1:T(2,128)(2,1)}, u32[]{:S(2)}) copy-start(bf16[2,430,256]{2,0,1:T(2,128)(2,1)} %param.9) | copy-start | bytes 1320964
  32.4 198.6 %copy-start.10 = (bf16[256,1024]{1,0:T(8,128)(2,1)S(1)}, bf16[256,1024]{1,0:T(8,128)(2,1)}, u32[]{:S(2)}) copy-start(bf16[256,1024]{1,0:T(8,128)(2,1)} %param.16) | copy-start | bytes 1572868
  32.4 391.8 %all-gather.3.cloned.1.call-start = ((), (), s32[]{:S(2)}) async-start(), calls=%async_computation.7 | async-start | bytes 3981312 | tf_op jit(solution)/shard_map/all_gather | solution.py:109
  348.9 166.8 %reduce-scatter.17.cloned.1.call-start = ((), (), s32[]{:S(2)}) async-start(), calls=%async_computation.10 | async-start | bytes 540672 | tf_op jit(solution)/shard_map/reduce_scatter | solution.py:163
  350.2 256.2 %reduce-scatter.23.cloned.1.call-start = ((), (), s32[]{:S(2)}) async-start(), calls=%async_computation.13 | async-start | bytes 1081344
  427.5 4.5 copy-start.4
  438.4 258.7 %reduce-scatter.21.cloned.1.call-start = ((), (), s32[]{:S(2)}) async-start(), calls=%async_computation.12 | async-start | bytes 1081344
  455.3 332.5 %reduce-scatter.19.cloned.1.call-start = ((), (), s32[]{:S(2)}) async-start(), calls=%async_computation.11 | async-start | bytes 1081344
  468.7 5.2 copy-start.6
  468.7 409.9 %reduce-scatter.15.cloned.1.call-start = ((), (), s32[]{:S(2)}) async-start(), calls=%async_computation.9 | async-start | bytes 1081344 | tf_op jit(solution)/shard_map/reduce_scatter | solution.py:160
  473.7 488.7 %reduce-scatter.13.cloned.1.call-start = ((), (), s32[]{:S(2)}) async-start(), calls=%async_computation.8 | async-start | bytes 3981312 | tf_op jit(solution)/shard_map/reduce_scatter | solution.py:144
  474.0 1.2 copy-start.8
  475.2 1.2 copy-start.9
Sparse Core Ops, SparseCore 0:
  32.5 167.8 all-reduce.3
  349.0 75.1 all-gather.2
  427.9 87.7 reduce-scatter.16
  519.4 86.9 reduce-scatter.22
  610.0 87.0 reduce-scatter.20
  700.7 87.0 reduce-scatter.18
  791.6 87.0 reduce-scatter.14
  881.2 81.0 reduce-scatter.12
where the time goes:
time: 982 us; the launch traced here: 973 us
  waiting for transfers between devices  665 us (68%)
  blocking collectives  186 us (19%)
  matrix products  72.4 us (7%)
  between operations  18.5 us (2%)
  other arithmetic  15 us (2%)
  local copies, waits for them, and re-layouts  14.2 us (1%)
    unnamed x11, waiting for transfers between devices  268 us
    psum x1, waiting for transfers between devices, local(): lax.psum(partial_value.astype(jnp.bfloat16), 'tensor').astype(jnp.float32)  117 us
    reduce_scatter x1, waiting for transfers between devices, local(): lax.psum_scatter(grad_out.astype(jnp.bfloat16), 'dp', scatter_dimension=1...  89.2 us
    psum x1, blocking collectives, local(): lax.psum((jnp.sum(exp_logits, axis=0), local_loss), 'dp')  83 us
    reduce_scatter x1, waiting for transfers between devices, local(): lax.psum_scatter(back_input.astype(jnp.bfloat16), 'tensor', scatter_dimen...  82.3 us
    all_gather x1, waiting for transfers between devices, local(): piece_rows = lax.all_gather(grad_resid, 'tensor', axis=2, tiled=True)  73.9 us
    all_gather x1, blocking collectives, local(): lax.all_gather(images, 'dp', axis=0, tiled=True).astype(jnp.float32)  50.5 us
    reduce_scatter x1, waiting for transfers between devices, local(): lax.psum_scatter(grad_proj.astype(jnp.bfloat16), 'dp', scatter_dimension=...  35 us
  transfers between devices with their start and end apart: 8, of which 8 were waited for; matrix products, arithmetic and copies ran while one was open for 6% of the time, Pallas kernels for 0%

commit v1 on v0

--- a/solution.py
+++ b/solution.py
@@ -56,7 +56,9 @@
     partial_value = jnp.einsum(
         "blc,cd->bld", head_concat, out_weight, preferred_element_type=jnp.float32
     )
-    summed = lax.psum(partial_value.astype(jnp.bfloat16), "tensor").astype(jnp.float32)
+    summed = jnp.sum(lax.all_gather(partial_value.astype(jnp.bfloat16), "tensor"), axis=0).astype(
+        jnp.float32
+    )
     attended = lax.dynamic_slice_in_dim(
         summed, lax.axis_index("tensor") * feat_share, feat_share, 2
     )

time: 982 us -> 1380 us (1.41)
  waiting for transfers between devices: 665 us -> 1050 us
    all_gather x0 -> x1, waiting for transfers between devices: none -> 499 us  [local(): lax.all_gather(partial_value.astype(jnp.bfloat16), 'tensor')]
    psum x1 -> x0, waiting for transfers between devices: 117 us -> none  [local(): lax.psum(partial_value.astype(jnp.bfloat16), 'tensor').astype(jnp.float32)]
  transfers between devices with their start and end apart: 8 -> 8, of which waited for: 8 -> 8; matrix products, arithmetic and copies ran while one was open for 6% -> 4% of each run, Pallas kernels for 0% -> 0%
where the time goes in v1:
time: 1380 us; the launch traced here: 1370 us
  waiting for transfers between devices  1050 us (76%)
  blocking collectives  188 us (14%)
  matrix products  70.7 us (5%)
  other arithmetic  28.4 us (2%)
  between operations  18.5 us (1%)
  local copies, waits for them, and re-layouts  16 us (1%)
    all_gather x1, waiting for transfers between devices, local(): lax.all_gather(partial_value.astype(jnp.bfloat16), 'tensor')  499 us
    unnamed x11, waiting for transfers between devices  268 us
    reduce_scatter x1, waiting for transfers between devices, local(): lax.psum_scatter(grad_out.astype(jnp.bfloat16), 'dp', scatter_dimension=1...  89.2 us
    psum x1, blocking collectives, local(): lax.psum((jnp.sum(exp_logits, axis=0), local_loss), 'dp')  82.7 us
    reduce_scatter x1, waiting for transfers between devices, local(): lax.psum_scatter(back_input.astype(jnp.bfloat16), 'tensor', scatter_dimen...  82.3 us
    all_gather x1, waiting for transfers between devices, local(): piece_rows = lax.all_gather(grad_resid, 'tensor', axis=2, tiled=True)  74 us
    all_gather x1, blocking collectives, local(): lax.all_gather(images, 'dp', axis=0, tiled=True).astype(jnp.float32)  50.4 us
    reduce_scatter x1, waiting for transfers between devices, local(): lax.psum_scatter(grad_proj.astype(jnp.bfloat16), 'dp', scatter_dimension=...  36.6 us
  transfers between devices with their start and end apart: 8, of which 8 were waited for; matrix products, arithmetic and copies ran while one was open for 4% of the time, Pallas kernels for 0%

profile of v1, /device:TPU:1, one launch (start us, length us, event | category | flops | bytes accessed | tf_op | source)
XLA Modules:
  0.0 1370.2 jit_solution(9700599846185294531)
XLA Ops:
  7.2 4.5 fusion.42
  11.9 4.0 fusion.45
  16.0 0.6 fusion.81
  16.7 2.9 fusion.122
  19.6 0.6 copy-done.3
  20.3 1.0 copy-done.2
  21.5 2.0 fusion.39
  23.7 4.7 fusion.48
  28.4 0.3 copy.70
  29.1 2.9 convolution_convert_fusion
  32.1 50.4 %all-gather.1 = bf16[32,2,1024]{2,1,0:T(2,128)(2,1)S(1)} all-gather(bf16[1,2,1024]{2,1,0:T(2,128)(2,1)S(1)} %bitcast.74), channel_id=1, replica_groups=mesh['dp'=32,'tensor'=8] {'dp'}, dimensions={0}, use_global_device_ids=true | all-gather | bytes 135168 | tf_op jit(solution)/shard_map/all_gather | solution.py:76
  82.7 498.6 %all-gather.7.cloned.1.call-done = bf16[16,430,2048]{2,1,0:T(8,128)(2,1)} async-done(((bf16[2,430,2048]{2,1,0:T(8,128)(2,1)}), bf16[16,430,2048]{2,1,0:T(8,128)(2,1)}) %all-gather.7.cloned.1.call-update) | async-done | bytes 28180496 | tf_op jit(solution)/shard_map/all_gather | solution.py:59
  581.2 13.4 reduce_sum.152
  594.6 1.2 fusion.73
  595.9 14.4 %psum.49 = f32[2,430]{1,0:T(2,128)S(1)} all-reduce(f32[2,430]{1,0:T(2,128)S(1)} %fusion.73), channel_id=1, replica_groups=mesh['dp'=32,'tensor'=8] {'tensor'}, use_global_device_ids=true, to_apply=%region_4.0 | all-reduce | flops 860 | bytes 6880 | tf_op jit(solution)/shard_map/psum | solution.py:66
  610.3 1.4 multiply_reduce_fusion.4
  611.6 12.6 psum.50
  624.2 1.3 multiply_reduce_fusion.3
  625.5 1.2 fusion.102
  626.8 14.6 %psum.51 = f32[2,1024]{1,0:T(2,128)S(1)} all-reduce(f32[2,1024]{1,0:T(2,128)S(1)} %fusion.102), channel_id=1, replica_groups=mesh['dp'=32,'tensor'=8] {'tensor'}, use_global_device_ids=true, to_apply=%region_8.0 | all-reduce | flops 2048 | bytes 16384 | tf_op jit(solution)/shard_map/psum | solution.py:73
  641.5 1.0 exponential_reduce_fusion
  642.5 0.6 fusion.120
  644.5 82.7 %all-reduce = (f32[64]{0:T(128)S(1)}, f32[]{:T(128)}) all-reduce(f32[64]{0:T(128)S(1)} %get-tuple-element.30, f32[]{:T(128)S(6)} %sub.68), channel_id=1, replica_groups=mesh['dp'=32,'tensor'=8] {'dp'}, use_global_device_ids=true, to_apply=%region_16.0 | all-reduce | flops 65 | bytes 520 | tf_op jit(solution)/shard_map/psum | solution.py:87
  727.1 0.6 fusion.121
  727.7 0.4 multiply_reduce_fusion.6
  728.2 1.3 convolution_multiply_fusion.1
  729.5 1.6 multiply_reduce_fusion.2
  731.1 12.9 all-reduce.1
  744.0 2.3 fusion.68
  746.4 1.2 convolution_convert_fusion.1
  747.7 74.0 %all-gather.5.cloned.1.call-done = bf16[2,430,2048]{2,1,0:T(8,128)(2,1)} async-done(((bf16[2,430,256]{2,1,0:T(8,128)(2,1)}), bf16[2,430,2048]{2,1,0:T(8,128)(2,1)}) %all-gather.5.cloned.1.call-update) | async-done | bytes 3522576 | tf_op jit(solution)/shard_map/all_gather | solution.py:111
  821.8 3.1 convolution_convert_fusion.3
  825.0 4.4 fusion.49
  829.4 0.3 copy.79
  830.0 4.4 fusion.12
  834.5 1.3 copy.93
  836.0 2.4 fusion.76
  838.5 6.6 fusion.50
  845.1 0.3 copy.77
  845.7 4.4 fusion.13
  850.2 1.4 copy.91
  851.6 7.0 fusion.53
  858.6 0.3 copy.75
  859.2 4.5 fusion.14
  863.7 1.3 copy.89
  865.1 4.7 fusion.11
  870.1 1.1 fusion.58
  871.3 1.1 fusion.61
  872.5 2.9 add_convert_fusion
  876.8 36.6 %reduce-scatter.17.cloned.1.call-done = bf16[256,32]{0,1:T(8,128)(2,1)} async-done(((bf16[256,1024]{0,1:T(8,128)(2,1)}), bf16[256,32]{0,1:T(8,128)(2,1)}) %reduce-scatter.17.cloned.1.call-update) | async-done | bytes 16400 | tf_op jit(solution)/shard_map/reduce_scatter | solution.py:165
  913.3 1.3 convert_element_type.149
  914.6 89.4 %reduce-scatter.23.cloned.1.call-done = bf16[64,256]{1,0:T(8,128)(2,1)} async-done(((bf16[2048,256]{1,0:T(8,128)(2,1)}), bf16[64,256]{1,0:T(8,128)(2,1)}) %reduce-scatter.23.cloned.1.call-update) | async-done | bytes 32784
  1004.0 0.9 copy.94
  1004.9 0.7 copy.86
  1005.6 89.1 %reduce-scatter.21.cloned.1.call-done = bf16[64,256]{1,0:T(8,128)(2,1)} async-done(((bf16[2048,256]{1,0:T(8,128)(2,1)}), bf16[64,256]{1,0:T(8,128)(2,1)}) %reduce-scatter.21.cloned.1.call-update) | async-done | bytes 32784
  1094.7 0.9 copy.92
  1095.6 0.7 copy.85
  1096.3 89.1 %reduce-scatter.19.cloned.1.call-done = bf16[64,256]{1,0:T(8,128)(2,1)} async-done(((bf16[2048,256]{1,0:T(8,128)(2,1)}), bf16[64,256]{1,0:T(8,128)(2,1)}) %reduce-scatter.19.cloned.1.call-update) | async-done | bytes 32784
  1185.4 0.9 copy.90
  1186.3 0.7 copy.84
  1187.0 89.2 %reduce-scatter.15.cloned.1.call-done = bf16[256,64]{0,1:T(8,128)(2,1)} async-done(((bf16[256,2048]{0,1:T(8,128)(2,1)}), bf16[256,64]{0,1:T(8,128)(2,1)}) %reduce-scatter.15.cloned.1.call-update) | async-done | bytes 32784 | tf_op jit(solution)/shard_map/reduce_scatter | solution.py:162
  1276.2 1.4 convert_element_type.147
  1277.6 82.3 %reduce-scatter.13.cloned.1.call-done = bf16[2,430,256]{2,1,0:T(8,128)(2,1)} async-done(((bf16[2,430,2048]{2,1,0:T(8,128)(2,1)}), bf16[2,430,256]{2,1,0:T(8,128)(2,1)}) %reduce-scatter.13.cloned.1.call-update) | async-done | bytes 440336 | tf_op jit(solution)/shard_map/reduce_scatter | solution.py:146
  1359.9 2.1 copy.83
  (60 shorter events, 3.3 us)
Async XLA Ops:
  7.2 21.9 %copy-start = (bf16[256,2048]{1,0:T(8,128)(2,1)S(1)}, bf16[256,2048]{1,0:T(8,128)(2,1)}, u32[]{:S(2)}) copy-start(bf16[256,2048]{1,0:T(8,128)(2,1)} %param.14) | copy-start | bytes 3145732
  7.2 4.7 copy-start.7
  7.2 574.0 %all-gather.7.cloned.1.call-start = ((), (), s32[]{:S(2)}) async-start(), calls=%async_computation.10 | async-start | bytes 31850496 | tf_op jit(solution)/shard_map/all_gather | solution.py:59
  16.7 3.6 copy-start.3
  16.7 4.6 copy-start.2
  16.7 4.8 copy-start.10
  29.1 3.0 copy-start.5
  29.1 3.0 copy-start.13
  29.1 3.0 copy-start.12
  32.0 789.7 %all-gather.5.cloned.1.call-start = ((), (), s32[]{:S(2)}) async-start(), calls=%async_computation.6 | async-start | bytes 3981312 | tf_op jit(solution)/shard_map/all_gather | solution.py:111
  581.2 13.4 copy-start.4
  746.4 166.9 %reduce-scatter.17.cloned.1.call-start = ((), (), s32[]{:S(2)}) async-start(), calls=%async_computation.9 | async-start | bytes 540672 | tf_op jit(solution)/shard_map/reduce_scatter | solution.py:165
  747.7 256.3 %reduce-scatter.23.cloned.1.call-start = ((), (), s32[]{:S(2)}) async-start(), calls=%async_computation.13 | async-start | bytes 1081344
  835.8 258.9 %reduce-scatter.21.cloned.1.call-start = ((), (), s32[]{:S(2)}) async-start(), calls=%async_computation.12 | async-start | bytes 1081344
  851.6 333.8 %reduce-scatter.19.cloned.1.call-start = ((), (), s32[]{:S(2)}) async-start(), calls=%async_computation.11 | async-start | bytes 1081344
  859.2 5.9 copy-start.6
  865.1 5.1 copy-start.8
  865.1 411.2 %reduce-scatter.15.cloned.1.call-start = ((), (), s32[]{:S(2)}) async-start(), calls=%async_computation.8 | async-start | bytes 1081344 | tf_op jit(solution)/shard_map/reduce_scatter | solution.py:162
  869.8 1.4 copy-start.9
  869.9 490.1 %reduce-scatter.13.cloned.1.call-start = ((), (), s32[]{:S(2)}) async-start(), calls=%async_computation.7 | async-start | bytes 3981312 | tf_op jit(solution)/shard_map/reduce_scatter | solution.py:146
  871.3 1.2 copy-start.11
  872.5 489.6 %copy-start.1 = (bf16[256,2048]{1,0:T(8,128)(2,1)S(1)}, bf16[256,2048]{1,0:T(8,128)(2,1)}, u32[]{:S(2)}) copy-start(bf16[256,2048]{1,0:T(8,128)(2,1)} %param.14) | copy-start | bytes 3145732
Sparse Core Ops, SparseCore 0:
  32.1 549.0 all-gather.6
  746.5 75.2 all-gather.4
  825.5 87.7 reduce-scatter.16
  916.9 87.0 reduce-scatter.22
  1007.6 87.0 reduce-scatter.20
  1098.4 86.9 reduce-scatter.18
  1189.2 87.0 reduce-scatter.14
  1278.8 81.0 reduce-scatter.12
